TPU v7x, 512 devices: a whole 4x4x16 slice. The times are simulated.
512 devices in a mesh: template: 16 (over y, x_hi, core), fsdp: 16 (over z), dp: 2 (over x_lo).
Axes of the slice: x: 4 (x_hi: 2, x_lo: 2; x = x_hi * 2 + x_lo), y: 4, z: 16, core: 2. Of those that a mesh axis runs over, the one named last changes fastest.
Arguments:
- hidden: bfloat16 [16, 4096, 8192], P('template', ('fsdp', 'dp')), may hold values from -6 to 6
- target: bfloat16 [16, 4096, 512], P('template', ('fsdp', 'dp')), may hold values from -6 to 6
- weight: bfloat16 [16, 8192, 512], P('template', 'fsdp'), may hold values from -6 to 6
- gain: bfloat16 [16, 8192], P('template', 'fsdp'), may hold values from 0.099609375 to 1.8984375
Outputs:
- merged_weight: float32 [8192, 512], P(('fsdp', 'dp'))
- merged_gain: float32 [8192], P(('fsdp', 'dp'))
All inputs are finite; a program needn't handle non-finite values.
Results may differ from a plain program's by a relative error of at most 0.0018.
Values may be sent and summed in bfloat16 or wider, within the bound.
No kernel may reach another device: no remote copies, remote signals or barrier semaphores. Data moves between devices by JAX's collectives and lax.ppermute only.
A program may use at most 64 MiB of HBM per device.

v0:
```python
import math
import jax
import jax.numpy as jnp
from jax import lax
from jax.sharding import PartitionSpec as P


def body(hidden, target, weight, gain):
    token_batch = hidden[0]
    goal = target[0]
    w_shard = weight[0]
    g_shard = gain[0]
    width = token_batch.shape[1]
    scale = 1.0 / math.sqrt(width)
    merge_quotient = lax.rsqrt(
        jnp.mean(jnp.square(token_batch.astype(jnp.float32)), axis=1, keepdims=True) + 1e-05
    )
    w_full, complete_gain = (
        lax.all_gather(w_shard, "fsdp", axis=0, tiled=True),
        lax.all_gather(g_shard, "fsdp", axis=0, tiled=True),
    )
    normalized_activation = token_batch.astype(jnp.float32) * merge_quotient
    normalized_input = (normalized_activation * complete_gain.astype(jnp.float32)[None, :]).astype(
        jnp.bfloat16
    )
    values = jnp.dot(normalized_input, w_full, preferred_element_type=jnp.float32) * scale
    delta = (values - goal.astype(jnp.float32)).astype(jnp.bfloat16)
    backward_pass = (
        jnp.einsum("th,dh->td", delta, w_full, preferred_element_type=jnp.float32) * scale
    )
    gain_information = jnp.sum(jnp.square(backward_pass * normalized_activation), axis=0)
    sq_normed = jnp.square(normalized_input.astype(jnp.float32)).astype(jnp.bfloat16)
    sq_delta = jnp.square(delta.astype(jnp.float32)).astype(jnp.bfloat16)
    mine = width // lax.axis_size(("fsdp", "dp"))
    columns = lax.all_to_all(sq_normed, ("fsdp", "dp"), split_axis=1, concat_axis=0, tiled=True)
    fisher = jnp.einsum(
        "td,th->dh",
        columns,
        lax.all_gather(sq_delta, ("fsdp", "dp"), axis=0, tiled=True),
        preferred_element_type=jnp.float32,
    )
    gain_total = lax.psum(gain_information.astype(jnp.bfloat16), ("fsdp", "dp")).astype(jnp.float32)
    where = lax.axis_index(("fsdp", "dp")) * mine
    gain_information_sum = lax.dynamic_slice_in_dim(gain_total, where, mine, 0)
    offset = lax.axis_index("dp") * mine
    theta = lax.dynamic_slice_in_dim(w_shard, offset, mine, 0).astype(jnp.float32)
    gmine = lax.dynamic_slice_in_dim(g_shard, offset, mine, 0).astype(jnp.float32)
    weighted = fisher * theta
    gain_weighted = (gain_information_sum * gmine)[:, None]
    gain_column = gain_information_sum[:, None]
    num, den, gnum, gden = lax.psum((weighted, fisher, gain_weighted, gain_column), "template")
    return (num / den, gnum[:, 0] / gden[:, 0])


def solution(mesh):
    in_specs = (
        P("template", ("fsdp", "dp"), None),
        P("template", ("fsdp", "dp"), None),
        P("template", "fsdp", None),
        P("template", "fsdp"),
    )
    out_specs = (P(("fsdp", "dp"), None), P(("fsdp", "dp")))
    return jax.shard_map(body, mesh=mesh, in_specs=in_specs, out_specs=out_specs, check_vma=False)
```

profile of v0, /device:TPU:1, one launch (start us, length us, event | category | flops | bytes accessed | tf_op | source)
XLA Modules:
  0.0 532.3 jit_solution(14916185869821254216)
XLA Ops:
  7.2 0.0 copy-start
  7.2 0.0 all-gather.7.cloned.1.call-start
  7.2 0.7 all-gather.7.cloned.1.call-update
  7.9 30.4 %all-gather = bf16[1,8192]{1,0:T(2,128)(2,1)S(1)} all-gather(bf16[1,512]{1,0:T(2,128)(2,1)} %param.7), channel_id=2, replica_groups=mesh['template'=16,'fsdp'=16,'dp'=2] {'fsdp'}, dimensions={1}, use_global_device_ids=true | all-gather | bytes 17408 | tf_op jit(solution)/shard_map/all_gather | solution.py:20
  38.3 0.1 convert_reduce_fusion
  38.4 2.2 copy.7
  40.7 0.0 copy-done
  40.7 0.5 fusion.5
  41.2 0.0 copy-start.3
  41.2 3.9 multiply_convert_fusion.1
  45.1 6.8 %all-to-all-start = ((bf16[128,32,256]{2,0,1:T(8,128)(2,1)}), bf16[128,32,256]{2,0,1:T(8,128)(2,1)}, u32[]{:S(2)}, u32[]{:S(2)}) async-start(bf16[128,32,256]{2,0,1:T(8,128)(2,1)} %multiply_convert_fusion.1), calls=%async_computation | async-start | bytes 4194304 | tf_op jit(solution)/shard_map/all_to_all | solution.py:35
  52.0 0.0 all-gather.5.cloned.1.call-start
  52.1 159.3 %all-gather.7.cloned.1.call-done = bf16[1,8192,512]{2,1,0:T(8,128)(2,1)} async-done(((bf16[1,512,512]{2,1,0:T(8,128)(2,1)}), bf16[1,8192,512]{2,1,0:T(8,128)(2,1)}) %all-gather.7.cloned.1.call-update) | async-done | bytes 8388624 | tf_op jit(solution)/shard_map/all_gather | solution.py:19
  211.3 0.0 copy-done.3
  211.3 0.0 copy-start.2
  211.3 0.0 copy-start.1
  211.3 5.4 %multiply_convert_fusion.9 = (bf16[128,512]{1,0:T(8,128)(2,1)}, bf16[128,512]{1,0:T(8,128)(2,1)S(1)}) fusion(bf16[1,128,512]{2,1,0:T(8,128)(2,1)S(1)} %copy-done.3, bf16[1,8192,512]{2,1,0:T(8,128)(2,1)} %all-gather.7.cloned.1.call-done, bf16[1,128,8192]{2,1,0:T(8,128)(2,1)S(1)} %copy-done, f32[8192]{0:T(1024)S(1)} %bitcast.58, f32[128]{0:T(128)S(1)} %add_rsqrt_fusion), kind=kOutput, calls=%fused_computation.21 | convolution fusion | flops 1078394880 | bytes 10912256 | tf_op jit(solution)/shard_map/dot_general | solution.py:26
  216.8 0.0 all-gather.5.cloned.1.call-update
  216.8 0.0 all-reduce.4.cloned.1.call-start
  216.8 0.0 copy-done.2
  216.9 0.0 all-to-all-done
  216.9 119.9 %all-gather.5.cloned.1.call-done = bf16[4096,512]{1,0:T(8,128)(2,1)} async-done(((bf16[128,512]{1,0:T(8,128)(2,1)}), bf16[4096,512]{1,0:T(8,128)(2,1)}) %all-gather.5.cloned.1.call-update) | async-done | bytes 4194320 | tf_op jit(solution)/shard_map/all_gather | solution.py:39
  336.8 0.0 copy-done.1
  336.8 5.1 convert_multiply_fusion
  341.8 0.0 all-reduce.4.cloned.1.call-update
  341.9 6.2 %fusion.10 = bf16[8192]{0:T(1024)(128)(2,1)S(1)} fusion(f32[128]{0:T(128)S(1)} %add_rsqrt_fusion, bf16[1,128,8192]{2,1,0:T(8,128)(2,1)S(1)} %copy-done, bf16[128,512]{1,0:T(8,128)(2,1)S(1)} %get-tuple-element.7, bf16[1,8192,512]{2,1,0:T(8,128)(2,1)} %all-gather.7.cloned.1.call-done), kind=kOutput, calls=%fused_computation.16 | convolution fusion | flops 1080025088 | bytes 10633728 | tf_op jit(solution)/shard_map/th,dh->td/dot_general | solution.py:29
  348.1 95.7 %psum.37 = bf16[8192]{0:T(1024)(128)(2,1)S(1)} all-reduce(bf16[8192]{0:T(1024)(128)(2,1)S(1)} %fusion.10), channel_id=1, replica_groups=mesh['template'=16,'fsdp'=16,'dp'=2] {'fsdp','dp'}, use_global_device_ids=true, to_apply=%region_4.0 | all-reduce | flops 8192 | bytes 32768 | tf_op jit(solution)/shard_map/psum | solution.py:42
  443.8 0.1 dynamic-slice_convert_fusion.1
  443.9 0.1 fusion.22
  443.9 79.2 %all-reduce = (f32[256,1]{0,1:T(1,128)S(1)}, f32[256,1]{0,1:T(1,128)S(1)}) all-reduce(f32[256,1]{0,1:T(1,128)S(1)} %bitcast.60, f32[256,1]{0,1:T(1,128)S(1)} %bitcast.61), channel_id=1, replica_groups=mesh['template'=16,'fsdp'=16,'dp'=2] {'template'}, use_global_device_ids=true, to_apply=%region_5.0 | all-reduce | flops 512 | bytes 4096 | tf_op jit(solution)/shard_map/psum | solution.py:51
  523.1 0.6 div.18
  523.7 0.0 all-reduce.4.cloned.1.call-done
  523.7 2.1 div.17
  (4 shorter events, 0.1 us)
Async XLA Ops:
  7.2 33.5 %copy-start = (bf16[1,128,8192]{2,1,0:T(8,128)(2,1)S(1)}, bf16[1,128,8192]{2,1,0:T(8,128)(2,1)}, u32[]{:S(2)}) copy-start(bf16[1,128,8192]{2,1,0:T(8,128)(2,1)} %param.4) | copy-start | bytes 6291460
  7.2 204.2 %all-gather.7.cloned.1.call-start = ((), (), s32[]{:S(2)}) async-start(), calls=%async_computation.2 | async-start | bytes 8912896 | tf_op jit(solution)/shard_map/all_gather | solution.py:19
  41.2 170.1 %copy-start.3 = (bf16[1,128,512]{2,1,0:T(8,128)(2,1)S(1)}, bf16[1,128,512]{2,1,0:T(8,128)(2,1)}, u32[]{:S(2)}) copy-start(bf16[1,128,512]{2,1,0:T(8,128)(2,1)} %param.5) | copy-start | bytes 393220
  45.1 171.7 %all-to-all-start = ((bf16[128,32,256]{2,0,1:T(8,128)(2,1)}), bf16[128,32,256]{2,0,1:T(8,128)(2,1)}, u32[]{:S(2)}, u32[]{:S(2)}) async-start(bf16[128,32,256]{2,0,1:T(8,128)(2,1)} %multiply_convert_fusion.1), calls=%async_computation | async-start | bytes 4194304 | tf_op jit(solution)/shard_map/all_to_all | solution.py:35
  52.0 284.8 %all-gather.5.cloned.1.call-start = ((), (), s32[]{:S(2)}) async-start(), calls=%async_computation.1 | async-start | bytes 4325376 | tf_op jit(solution)/shard_map/all_gather | solution.py:39
  211.3 5.5 %copy-start.2 = (bf16[1,512]{1,0:T(2,128)(2,1)S(1)}, bf16[1,512]{1,0:T(2,128)(2,1)}, u32[]{:S(2)}) copy-start(bf16[1,512]{1,0:T(2,128)(2,1)} %param.7) | copy-start | bytes 3076
  211.3 125.4 %copy-start.1 = (bf16[1,512,512]{2,1,0:T(8,128)(2,1)S(1)}, bf16[1,512,512]{2,1,0:T(8,128)(2,1)}, u32[]{:S(2)}) copy-start(bf16[1,512,512]{2,1,0:T(8,128)(2,1)} %param.6) | copy-start | bytes 1572868
  216.8 306.9 %all-reduce.4.cloned.1.call-start = ((), (), s32[]{:S(2)}) async-start(), calls=%async_computation.3 | async-start | bytes 2097152 | tf_op jit(solution)/shard_map/psum | solution.py:51
Sparse Core Ops, SparseCore 0:
  10.1 201.2 all-gather.6
  216.9 119.8 all-gather.4
  342.0 171.5 all-reduce.3
where the time goes:
time: 533 us; the launch traced here: 532 us
  waiting for transfers between devices  280 us (53%)
  blocking collectives  205 us (38%)
  matrix products  16.7 us (3%)
  between operations  13.8 us (3%)
  other arithmetic  7.36 us (1%)
  starting transfers between devices  6.94 us (1%)
    all_gather x1, waiting for transfers between devices, body(): lax.all_gather(w_shard, 'fsdp', axis=0, tiled=True)  159 us
    all_gather x1, waiting for transfers between devices, body(): lax.all_gather(sq_delta, ('fsdp', 'dp'), axis=0, tiled=True)  120 us
    psum x1, blocking collectives, body(): lax.psum(gain_information.astype(jnp.bfloat16), ('fsdp', 'dp'))  95.7 us
    psum x1, blocking collectives, body(): lax.psum((weighted, fisher, gain_weighted, gain_column), 'template')  79.2 us
    all_gather x1, blocking collectives, body(): lax.all_gather(g_shard, 'fsdp', axis=0, tiled=True)  30.4 us
  transfers between devices with their start and end apart: 4, of which 2 were waited for; matrix products, arithmetic and copies ran while one was open for 4% of the time, Pallas kernels for 0%

commit v1 on v0

--- a/solution.py
+++ b/solution.py
@@ -16,7 +16,9 @@
         jnp.mean(jnp.square(token_batch.astype(jnp.float32)), axis=1, keepdims=True) + 1e-05
     )
     w_full, complete_gain = (
-        lax.all_gather(w_shard, "fsdp", axis=0, tiled=True),
+        jnp.concatenate(
+            lax.all_to_all(jnp.stack([w_shard] * lax.axis_size("fsdp")), "fsdp", 0, 0), axis=0
+        ),
         lax.all_gather(g_shard, "fsdp", axis=0, tiled=True),
     )
     normalized_activation = token_batch.astype(jnp.float32) * merge_quotient

time: 533 us -> 789 us (1.48)
  blocking collectives: 205 us -> 549 us
  waiting for transfers between devices: 280 us -> 168 us
  starting transfers between devices: 6.94 us -> 27.4 us
    all_gather x1, blocking collectives: 30.4 us -> 380 us  [body(): lax.all_gather(g_shard, 'fsdp', axis=0, tiled=True)]
    all_gather x1 -> x0, waiting for transfers between devices: 159 us -> none  [body(): lax.all_gather(w_shard, 'fsdp', axis=0, tiled=True)]
    all_to_all x1, waiting for transfers between devices: 0.01 us -> 90.3 us  [body(): lax.all_to_all(sq_normed, ('fsdp', 'dp'), split_axis=1, concat_axis=0, ti...]
    all_gather x1, waiting for transfers between devices: 120 us -> 77.4 us  [body(): lax.all_gather(sq_delta, ('fsdp', 'dp'), axis=0, tiled=True)]
    all_to_all x0 -> x1, starting transfers between devices: none -> 15.9 us  [body(): lax.all_to_all(jnp.stack([w_shard] * lax.axis_size('fsdp')), 'fsdp', 0, 0)]
  transfers between devices with their start and end apart: 4 -> 4, of which waited for: 2 -> 2; matrix products, arithmetic and copies ran while one was open for 4% -> 2% of each run, Pallas kernels for 0% -> 0%
where the time goes in v1:
time: 789 us; the launch traced here: 788 us
  blocking collectives  549 us (70%)
  waiting for transfers between devices  168 us (21%)
  starting transfers between devices  27.4 us (3%)
  matrix products  16.7 us (2%)
  between operations  14.2 us (2%)
    all_gather x1, blocking collectives, body(): lax.all_gather(g_shard, 'fsdp', axis=0, tiled=True)  380 us
    psum x1, blocking collectives, body(): lax.psum(gain_information.astype(jnp.bfloat16), ('fsdp', 'dp'))  96.7 us
    all_to_all x1, waiting for transfers between devices, body(): lax.all_to_all(sq_normed, ('fsdp', 'dp'), split_axis=1, concat_axis=0, ti...  90.3 us
    all_gather x1, waiting for transfers between devices, body(): lax.all_gather(sq_delta, ('fsdp', 'dp'), axis=0, tiled=True)  77.4 us
    psum x1, blocking collectives, body(): lax.psum((weighted, fisher, gain_weighted, gain_column), 'template')  72.9 us
    all_to_all x1, starting transfers between devices, body(): lax.all_to_all(jnp.stack([w_shard] * lax.axis_size('fsdp')), 'fsdp', 0, 0)  15.9 us
  transfers between devices with their start and end apart: 4, of which 2 were waited for; matrix products, arithmetic and copies ran while one was open for 2% of the time, Pallas kernels for 0%

profile of v1, /device:TPU:1, one launch (start us, length us, event | category | flops | bytes accessed | tf_op | source)
XLA Modules:
  0.0 788.5 jit_solution(313509841944739413)
XLA Ops:
  7.2 5.1 stack.3
  12.2 0.0 copy-start.2
  12.2 0.0 copy-start
  12.2 15.9 %all-to-all-start.1 = ((bf16[16,512,512]{2,1,0:T(8,128)(2,1)}), bf16[16,512,512]{2,1,0:T(8,128)(2,1)}, u32[]{:S(2)}, u32[]{:S(2)}) async-start(bf16[16,512,512]{2,1,0:T(8,128)(2,1)} %stack.3), calls=%async_computation.1 | async-start | bytes 16777216 | tf_op jit(solution)/shard_map/all_to_all | solution.py:20
  28.2 0.0 copy-done.2
  28.2 379.9 %all-gather = bf16[1,8192]{1,0:T(2,128)(2,1)S(1)} all-gather(bf16[1,512]{1,0:T(2,128)(2,1)S(1)} %copy-done.2), channel_id=2, replica_groups=mesh['template'=16,'fsdp'=16,'dp'=2] {'fsdp'}, dimensions={1}, use_global_device_ids=true | all-gather | bytes 17408 | tf_op jit(solution)/shard_map/all_gather | solution.py:22
  408.1 0.1 convert_reduce_fusion
  408.3 0.0 copy-done
  408.3 0.6 copy.7
  408.9 0.5 fusion.2
  409.4 0.0 copy-start.3
  409.4 3.9 multiply_convert_fusion.1
  413.4 0.0 all-to-all-done.1
  413.4 11.3 %all-to-all-start = ((bf16[128,32,256]{2,0,1:T(8,128)(2,1)}), bf16[128,32,256]{2,0,1:T(8,128)(2,1)}, u32[]{:S(2)}, u32[]{:S(2)}) async-start(bf16[128,32,256]{2,0,1:T(8,128)(2,1)} %multiply_convert_fusion.1), calls=%async_computation | async-start | bytes 4194304 | tf_op jit(solution)/shard_map/all_to_all | solution.py:37
  424.7 0.0 all-gather.3.cloned.1.call-start
  424.8 0.0 copy-done.3
  424.8 0.0 copy-start.1
  424.8 5.4 multiply_convert_fusion.2
  430.2 0.0 all-gather.3.cloned.1.call-update
  430.2 0.0 all-reduce.4.cloned.1.call-start
  430.3 90.3 %all-to-all-done = bf16[128,32,256]{2,0,1:T(8,128)(2,1)} async-done(((bf16[128,32,256]{2,0,1:T(8,128)(2,1)}), bf16[128,32,256]{2,0,1:T(8,128)(2,1)}, u32[]{:S(2)}, u32[]{:S(2)}) %all-to-all-start) | async-done | bytes 2097184 | tf_op jit(solution)/shard_map/all_to_all | solution.py:37
  520.6 77.4 %all-gather.3.cloned.1.call-done = bf16[4096,512]{1,0:T(8,128)(2,1)} async-done(((bf16[128,512]{1,0:T(8,128)(2,1)}), bf16[4096,512]{1,0:T(8,128)(2,1)}) %all-gather.3.cloned.1.call-update) | async-done | bytes 4194320 | tf_op jit(solution)/shard_map/all_gather | solution.py:41
  598.0 0.0 copy-done.1
  598.0 5.1 convert_multiply_fusion
  603.0 0.0 all-reduce.4.cloned.1.call-update
  603.1 6.2 fusion.10
  609.3 96.7 %psum.37 = bf16[8192]{0:T(1024)(128)(2,1)S(1)} all-reduce(bf16[8192]{0:T(1024)(128)(2,1)S(1)} %fusion.10), channel_id=1, replica_groups=mesh['template'=16,'fsdp'=16,'dp'=2] {'fsdp','dp'}, use_global_device_ids=true, to_apply=%region_4.0 | all-reduce | flops 8192 | bytes 32768 | tf_op jit(solution)/shard_map/psum | solution.py:44
  706.0 0.1 dynamic-slice_convert_fusion.1
  706.0 0.1 fusion.20
  706.1 72.9 %all-reduce = (f32[256,1]{0,1:T(1,128)S(1)}, f32[256,1]{0,1:T(1,128)S(1)}) all-reduce(f32[256,1]{0,1:T(1,128)S(1)} %bitcast.50, f32[256,1]{0,1:T(1,128)S(1)} %bitcast.51), channel_id=1, replica_groups=mesh['template'=16,'fsdp'=16,'dp'=2] {'template'}, use_global_device_ids=true, to_apply=%region_5.0 | all-reduce | flops 512 | bytes 4096 | tf_op jit(solution)/shard_map/psum | solution.py:53
  779.0 0.6 div.18
  779.6 0.0 all-reduce.4.cloned.1.call-done
  779.6 2.1 div.17
  (4 shorter events, 0.1 us)
Async XLA Ops:
  12.2 15.9 %copy-start.2 = (bf16[1,512]{1,0:T(2,128)(2,1)S(1)}, bf16[1,512]{1,0:T(2,128)(2,1)}, u32[]{:S(2)}) copy-start(bf16[1,512]{1,0:T(2,128)(2,1)} %param.7) | copy-start | bytes 3076
  12.2 396.0 %copy-start = (bf16[1,128,8192]{2,1,0:T(8,128)(2,1)S(1)}, bf16[1,128,8192]{2,1,0:T(8,128)(2,1)}, u32[]{:S(2)}) copy-start(bf16[1,128,8192]{2,1,0:T(8,128)(2,1)} %param.4) | copy-start | bytes 6291460
  12.2 401.1 %all-to-all-start.1 = ((bf16[16,512,512]{2,1,0:T(8,128)(2,1)}), bf16[16,512,512]{2,1,0:T(8,128)(2,1)}, u32[]{:S(2)}, u32[]{:S(2)}) async-start(bf16[16,512,512]{2,1,0:T(8,128)(2,1)} %stack.3), calls=%async_computation.1 | async-start | bytes 16777216 | tf_op jit(solution)/shard_map/all_to_all | solution.py:20
  409.4 15.4 %copy-start.3 = (bf16[1,128,512]{2,1,0:T(8,128)(2,1)S(1)}, bf16[1,128,512]{2,1,0:T(8,128)(2,1)}, u32[]{:S(2)}) copy-start(bf16[1,128,512]{2,1,0:T(8,128)(2,1)} %param.5) | copy-start | bytes 393220
  413.4 107.2 %all-to-all-start = ((bf16[128,32,256]{2,0,1:T(8,128)(2,1)}), bf16[128,32,256]{2,0,1:T(8,128)(2,1)}, u32[]{:S(2)}, u32[]{:S(2)}) async-start(bf16[128,32,256]{2,0,1:T(8,128)(2,1)} %multiply_convert_fusion.1), calls=%async_computation | async-start | bytes 4194304 | tf_op jit(solution)/shard_map/all_to_all | solution.py:37
  424.7 173.3 %all-gather.3.cloned.1.call-start = ((), (), s32[]{:S(2)}) async-start(), calls=%async_computation.2 | async-start | bytes 4325376 | tf_op jit(solution)/shard_map/all_gather | solution.py:41
  424.8 173.2 %copy-start.1 = (bf16[1,512,512]{2,1,0:T(8,128)(2,1)S(1)}, bf16[1,512,512]{2,1,0:T(8,128)(2,1)}, u32[]{:S(2)}) copy-start(bf16[1,512,512]{2,1,0:T(8,128)(2,1)} %param.6) | copy-start | bytes 1572868
  430.2 349.3 %all-reduce.4.cloned.1.call-start = ((), (), s32[]{:S(2)}) async-start(), calls=%async_computation.3 | async-start | bytes 2097152 | tf_op jit(solution)/shard_map/psum | solution.py:53
Sparse Core Ops, SparseCore 0:
  430.4 167.5 all-gather.2
  603.2 166.4 all-reduce.3
